TPU v7x, 32 devices: a whole 2x2x4 slice. The times are simulated.
32 devices in a mesh: parts: 2 (over y), ctx: 8 (over z, x), tp: 2 (over core).
Axes of the slice: x: 2, y: 2, z: 4, core: 2. Of those that a mesh axis runs over, the one named last changes fastest.
Arguments:
- queries: bfloat16 [2048, 8192], P(('parts', 'ctx'), 'tp'), parts along dimension 0, may hold values from -9 to 9
- episode_key_cache: bfloat16 [128, 16, 1024], P(None, ('parts', 'ctx'), 'tp'), parts along dimension 1, may hold values from -9 to 9
- episode_value_cache: bfloat16 [128, 16, 1024], P(None, ('parts', 'ctx'), 'tp'), parts along dimension 1, may hold values from -6 to 6
- output_gradient: bfloat16 [2048, 8192], P(('parts', 'ctx'), 'tp'), parts along dimension 0, may hold values from -6 to 6
- block_lists: int32 [16, 2], P(('parts', 'ctx')), parts along dimension 0, may hold values from 0 to 7, as said below
- block_counts: int32 [16], P(('parts', 'ctx')), parts along dimension 0, may hold values from 1 to 2
Outputs:
- attn_out: bfloat16 [2048, 8192], P(('parts', 'ctx'), 'tp'), parts along dimension 0
- query_grad: bfloat16 [2048, 8192], P(('parts', 'ctx'), 'tp'), parts along dimension 0
- key_cache_gradient: bfloat16 [128, 16, 1024], P(None, ('parts', 'ctx'), 'tp'), parts along dimension 1
- value_cache_gradient: bfloat16 [128, 16, 1024], P(None, ('parts', 'ctx'), 'tp'), parts along dimension 1
There are 2 independent parts, one for each index of `parts`. A program takes and returns all parts, laid end to end along the dimension named above; each array names one. Nothing has to cross between parts.
Inputs may be any that keep to these rules, and one draw needn't show every extreme that they name: `block_lists`: each row names 2 different key blocks; a query block reads only its first block_counts entries.
All inputs are finite; a program needn't handle non-finite values.
Results may differ from a plain program's by a relative error of at most 0.0085.
The roundings to bfloat16 on the way count: a program that leaves them out, or rounds other values in their place, can miss the bound.
Values may be sent and summed in bfloat16 or wider, within the bound.
No kernel may reach another device: no remote copies, remote signals or barrier semaphores. Data moves between devices by JAX's collectives and lax.ppermute only.
A program may use at most 64 MiB of HBM per device.

v0:
```python
import jax
import jax.numpy as jnp
from jax import lax
from jax.sharding import PartitionSpec as P

QUERY_HEADS = 64
KEY_VALUE_HEADS = 8
HEAD_SIZE = 128
LIST = 2
TAG_COLUMNS = 128


def attend(query_part, key_part, value_part, grad_part, live_slots):
    score_scale = HEAD_SIZE ** (-0.5)
    scores = score_scale * jnp.einsum(
        "qgah,jkgh->gaqjk", query_part, key_part, preferred_element_type=jnp.float32
    )
    masked = jnp.where(live_slots[None, None, None, :, None], scores, -jnp.inf)
    row_peak = jnp.max(masked, axis=(3, 4), keepdims=True)
    exponent = jnp.exp(masked - row_peak)
    weights = exponent / jnp.sum(exponent, axis=(3, 4), keepdims=True)
    weights_low = weights.astype(jnp.bfloat16)
    attended = jnp.einsum(
        "gaqjk,jkgh->qgah", weights_low, value_part, preferred_element_type=jnp.float32
    ).astype(jnp.bfloat16)
    attended = lax.optimization_barrier(attended)
    row_delta = jnp.sum(grad_part.astype(jnp.float32) * attended.astype(jnp.float32), axis=3)
    weight_grad = jnp.einsum(
        "qgah,jkgh->gaqjk", grad_part, value_part, preferred_element_type=jnp.float32
    )
    score_grad = (
        weights * (weight_grad - jnp.transpose(row_delta, (1, 2, 0))[:, :, :, None, None])
    ).astype(jnp.bfloat16)
    query_grad = (
        score_scale
        * jnp.einsum("gaqjk,jkgh->qgah", score_grad, key_part, preferred_element_type=jnp.float32)
    ).astype(jnp.bfloat16)
    key_piece = score_scale * jnp.einsum(
        "gaqjk,qgah->jkgh", score_grad, query_part, preferred_element_type=jnp.float32
    )
    value_piece = jnp.einsum(
        "gaqjk,qgah->jkgh", weights_low, grad_part, preferred_element_type=jnp.float32
    )
    return (attended, query_grad, key_piece, value_piece)


def make_shards(peers):

    def shards(
        queries, episode_key_cache, episode_value_cache, output_gradient, block_lists, block_counts
    ):
        row_count = episode_key_cache.shape[0]
        key_width = episode_key_cache.shape[2]
        both_width = 2 * key_width
        chunk_rows = row_count // peers
        local_groups = key_width // HEAD_SIZE
        queries_per_group = QUERY_HEADS // KEY_VALUE_HEADS
        query_rows = queries.shape[0]
        held = jnp.concatenate([episode_key_cache[:, 0, :], episode_value_cache[:, 0, :]], axis=1)
        tag = jnp.concatenate([block_lists[0], block_counts]).astype(jnp.bfloat16)
        tag_block = jnp.zeros((row_count, TAG_COLUMNS), jnp.bfloat16)
        tag_block = tag_block.at[:, : LIST + 1].set(jnp.broadcast_to(tag, (row_count, LIST + 1)))
        first_send = jnp.concatenate([held, tag_block], axis=1).reshape(
            peers, chunk_rows, both_width + TAG_COLUMNS
        )
        first_recv = lax.all_to_all(first_send, "ctx", 0, 0, tiled=True)
        info = first_recv[:, 0, both_width : both_width + LIST + 1].astype(jnp.int32)
        lists_all = info[:, :LIST]
        counts_all = info[:, LIST]
        rows_held = first_recv[:, :, :both_width]
        picked = jnp.take(rows_held, lists_all, axis=0, mode="clip")
        fetched = lax.all_to_all(picked, "ctx", 0, 2, tiled=True)[0]
        key_rows = fetched[:, :, :key_width].reshape(LIST, row_count, local_groups, HEAD_SIZE)
        value_rows = fetched[:, :, key_width:].reshape(LIST, row_count, local_groups, HEAD_SIZE)
        live_slots = jnp.arange(LIST, dtype=jnp.int32) < block_counts[0]
        query_part = queries.reshape(query_rows, local_groups, queries_per_group, HEAD_SIZE)
        grad_part = output_gradient.reshape(query_rows, local_groups, queries_per_group, HEAD_SIZE)
        attended, query_grad, key_piece, value_piece = attend(
            query_part, key_rows, value_rows, grad_part, live_slots
        )
        pieces = jnp.concatenate(
            [
                key_piece.reshape(LIST, row_count, key_width),
                value_piece.reshape(LIST, row_count, key_width),
            ],
            axis=2,
        ).astype(jnp.bfloat16)
        back = lax.all_to_all(
            pieces.reshape(LIST, peers, chunk_rows, both_width), "ctx", 1, 1, tiled=True
        )
        slot_live = jnp.arange(LIST, dtype=jnp.int32)[None, :] < counts_all[:, None]
        selector = (
            (lists_all[:, :, None] == jnp.arange(peers, dtype=jnp.int32)[None, None, :])
            & slot_live[:, :, None]
        ).astype(jnp.bfloat16)
        summed = jnp.einsum(
            "jqrc,qjn->nrc", back, selector, preferred_element_type=jnp.float32
        ).astype(jnp.bfloat16)
        owned = lax.all_to_all(summed, "ctx", 0, 0, tiled=True).reshape(row_count, both_width)
        key_cache_gradient = owned[:, None, :key_width]
        value_cache_gradient = owned[:, None, key_width:]
        attn_out = attended.reshape(query_rows, local_groups * queries_per_group * HEAD_SIZE)
        query_grad = query_grad.reshape(query_rows, local_groups * queries_per_group * HEAD_SIZE)
        return (attn_out, query_grad, key_cache_gradient, value_cache_gradient)

    return shards


def solution(mesh):
    placed = (
        P(("parts", "ctx"), "tp"),
        P(None, ("parts", "ctx"), "tp"),
        P(None, ("parts", "ctx"), "tp"),
        P(("parts", "ctx"), "tp"),
        P(("parts", "ctx"), None),
        P(("parts", "ctx")),
    )
    return jax.shard_map(
        make_shards(mesh.shape["ctx"]),
        mesh=mesh,
        in_specs=placed,
        out_specs=(
            P(("parts", "ctx"), "tp"),
            P(("parts", "ctx"), "tp"),
            P(None, ("parts", "ctx"), "tp"),
            P(None, ("parts", "ctx"), "tp"),
        ),
        check_vma=False,
    )
```

profile of v0, /device:TPU:0, one launch (start us, length us, event | category | flops | bytes accessed | tf_op | source)
XLA Modules:
  0.0 88.5 jit_solution(7649527728791196662)
XLA Ops:
  0.6 0.0 copy-start.1
  0.6 0.6 compare_reduce_fusion
  1.9 0.7 convert_bitcast_fusion
  2.6 0.7 broadcast_select_fusion
  3.3 1.0 %maximum_maximum_fusion = bf16[8,16,1152]{2,1,0:T(8,128)(2,1)S(1)} fusion(bf16[8,16,512]{2,1,0:T(8,128)(2,1)} %bitcast.124, bf16[8,16,512]{2,1,0:T(8,128)(2,1)} %bitcast.125, bf16[1152]{0:T(1024)(128)(2,1)S(1)} %fusion.34), kind=kLoop, calls=%fused_computation.33 | loop fusion | flops 884736 | bytes 559360 | tf_op jit(solution)/shard_map/concatenate | solution.py:63
  4.4 17.4 %all_to_all.30 = bf16[8,16,1152]{2,1,0:T(8,128)(2,1)S(1)} all-to-all(bf16[8,16,1152]{2,1,0:T(8,128)(2,1)S(1)} %maximum_maximum_fusion), channel_id=1, replica_groups=mesh['parts'=2,'ctx'=8,'tp'=2] {'ctx'}, dimensions={0} | all-to-all | bytes 589824 | tf_op jit(solution)/shard_map/all_to_all | solution.py:66
  21.8 0.1 copy.175
  21.9 0.1 copy.119
  22.0 0.1 reshape.111
  22.1 1.4 %gather_fusion = bf16[16,16,1024]{2,1,0:T(8,128)(2,1)} fusion(bf16[8,16,1024]{2,1,0:T(8,128)(2,1)S(1)} %slice.53, s32[1024]{0:T(1024)S(1)} %pad_clamp_fusion), kind=kCustom, calls=%fused_computation | custom fusion | bytes 1048640 | tf_op jit(solution)/shard_map/jit(_take)/gather | solution.py:71
  23.5 3.5 %all-to-all-start.1 = ((bf16[8,2,16,1024]{3,2,1,0:T(8,128)(2,1)}), bf16[8,2,16,1024]{3,2,1,0:T(8,128)(2,1)S(1)}, u32[]{:S(2)}, u32[]{:S(2)}) async-start(bf16[8,2,16,1024]{3,2,1,0:T(8,128)(2,1)} %bitcast.3), calls=%async_computation.1 | async-start | bytes 1048576 | tf_op jit(solution)/shard_map/all_to_all | solution.py:72
  27.0 0.0 copy-done.1
  27.0 0.7 copy.127
  27.7 1.4 %copy.176 = bf16[16,8,32,128]{3,2,1,0:T(8,128)(2,1)S(1)} copy(bf16[16,8,32,128]{3,1,2,0:T(8,128)(2,1)} %bitcast.119) | data formatting | bytes 2097152
  29.1 11.6 %all-to-all-done.1 = bf16[8,2,16,1024]{3,2,1,0:T(8,128)(2,1)S(1)} async-done(((bf16[8,2,16,1024]{3,2,1,0:T(8,128)(2,1)}), bf16[8,2,16,1024]{3,2,1,0:T(8,128)(2,1)S(1)}, u32[]{:S(2)}, u32[]{:S(2)}) %all-to-all-start.1) | async-done | bytes 524320 | tf_op jit(solution)/shard_map/all_to_all | solution.py:72
  40.8 0.8 copy.121
  41.7 0.2 copy.122
  41.9 1.1 %bitcast_reduce_fusion = (f32[4,8,128]{2,1,0:T(8,128)S(1)}, f32[4,2,128,128,8]{3,2,4,1,0:T(8,128)S(1)}) fusion(pred[2]{0:T(512)(128)(4,1)S(1)} %iota_compare_fusion.3, bf16[128,4,8,128,1]{3,2,1,0,4:T(8,128)(2,1)S(1)} %bitcast.113, bf16[2,128,4,128,1]{1,3,2,0,4:T(8,128)(2,1)S(1)} %bitcast.117), kind=kOutput, calls=%fused_computation.5 | convolution fusion | flops 271577088 | bytes 5521410 | tf_op jit(solution)/shard_map/qgah,jkgh->gaqjk/dot_general | solution.py:15
  42.9 0.0 copy-start
  42.9 1.0 %fusion.4 = f32[4,8,128]{2,1,0:T(8,128)S(1)} fusion(f32[4,2,128,128,8]{3,2,4,1,0:T(8,128)S(1)} %get-tuple-element.45, f32[4,8,128]{2,1,0:T(8,128)S(1)} %get-tuple-element.44, pred[2]{0:T(512)(128)(4,1)S(1)} %iota_compare_fusion.3), kind=kLoop, calls=%fused_computation.9 | loop fusion | flops 4190208 | bytes 4227074 | tf_op jit(solution)/shard_map/reduce_sum | solution.py:21
  43.9 0.0 copy-start.3
  43.9 1.1 %fusion.37 = bf16[4,8,128,2,128]{2,4,1,3,0:T(8,128)(2,1)S(1)} fusion(f32[4,8,128]{2,1,0:T(8,128)S(1)} %fusion.4, f32[4,8,128]{2,1,0:T(8,128)S(1)} %get-tuple-element.44, f32[4,2,128,128,8]{3,2,4,1,0:T(8,128)S(1)} %get-tuple-element.45, pred[2]{0:T(512)(128)(4,1)S(1)} %iota_compare_fusion.3), kind=kLoop, calls=%fused_computation.55 | loop fusion | flops 5242880 | bytes 6324226 | tf_op jit(solution)/shard_map/convert_element_type | solution.py:22
  45.0 0.0 copy-done
  45.0 0.7 fusion.21
  45.7 0.0 copy-done.3
  45.7 0.5 fusion.14
  46.2 0.9 %copy.135 = bf16[2,128,4,128]{3,2,1,0:T(4,128)(2,1)} copy(bf16[2,128,4,128]{3,1,0,2:T(8,128)(2,1)S(1)} %fusion.21) | data formatting | bytes 524288 | tf_op jit(solution)/shard_map/gaqjk,qgah->jkgh/transpose | solution.py:41
  47.1 1.7 %concatenate.31 = bf16[2,8,16,512]{3,2,1,0:T(8,128)(2,1)} reshape(bf16[2,128,4,128]{3,2,1,0:T(4,128)(2,1)} %copy.135) | data formatting | bytes 524288 | tf_op jit(solution)/shard_map/concatenate | solution.py:81
  48.8 0.4 multiply_reduce_fusion
  49.2 3.9 %fusion.1 = bf16[4,8,128,2,128]{2,4,1,3,0:T(8,128)(2,1)S(1)} fusion(bf16[128,4,8,128,1]{0,3,2,4,1:T(8,128)(2,1)S(1)} %bitcast.112, f32[4,8,128]{2,1,0:T(8,128)S(1)} %bitcast.126, bf16[2,128,4,128,1]{1,3,2,0,4:T(8,128)(2,1)} %bitcast.122, f32[4,8,128]{2,1,0:T(8,128)S(1)} %fusion.4, f32[4,8,128]{2,1,0:T(8,128)S(1)} %get-tuple-element.44, ...), kind=kOutput, calls=%fused_computation.3 | convolution fusion | flops 275775488 | bytes 7651330 | tf_op jit(solution)/shard_map/qgah,jkgh->gaqjk/dot_general | solution.py:28
  53.1 0.0 copy-start.4
  53.2 0.8 fusion.22
  54.0 0.5 copy-done.4
  54.5 0.2 copy.133
  54.7 0.1 concatenate.30
  54.8 0.0 copy-done.2
  54.8 0.1 pad_maximum_fusion
  54.9 1.3 %copy.136 = bf16[2,8,16,1024]{3,0,2,1:T(2,128)(2,1)} copy(bf16[2,8,16,1024]{3,2,1,0:T(8,128)(2,1)S(1)} %pad_maximum_fusion) | data formatting | bytes 1048576 | tf_op jit(solution)/shard_map/concatenate | solution.py:81
  56.2 3.6 %all-to-all-start.2 = ((bf16[2,8,16,1024]{3,0,2,1:T(2,128)(2,1)}), bf16[2,8,16,1024]{3,0,2,1:T(2,128)(2,1)S(1)}, u32[]{:S(2)}, u32[]{:S(2)}) async-start(bf16[2,8,16,1024]{3,0,2,1:T(2,128)(2,1)} %copy.136), calls=%async_computation.2 | async-start | bytes 1048576 | tf_op jit(solution)/shard_map/all_to_all | solution.py:88
  59.9 14.2 %all-to-all-done.2 = bf16[2,8,16,1024]{3,0,2,1:T(2,128)(2,1)S(1)} async-done(((bf16[2,8,16,1024]{3,0,2,1:T(2,128)(2,1)}), bf16[2,8,16,1024]{3,0,2,1:T(2,128)(2,1)S(1)}, u32[]{:S(2)}, u32[]{:S(2)}) %all-to-all-start.2) | async-done | bytes 524320 | tf_op jit(solution)/shard_map/all_to_all | solution.py:88
  74.0 0.4 fusion.20
  74.4 0.9 copy.138
  75.3 3.6 %all-to-all-start.3 = ((bf16[8,16,1024]{2,1,0:T(8,128)(2,1)}), bf16[8,16,1024]{2,1,0:T(8,128)(2,1)S(1)}, u32[]{:S(2)}, u32[]{:S(2)}) async-start(bf16[8,16,1024]{2,1,0:T(8,128)(2,1)} %copy.138), calls=%async_computation.3 | async-start | bytes 524288 | tf_op jit(solution)/shard_map/all_to_all | solution.py:99
  78.9 2.1 %fusion.5 = bf16[4,128,8,128]{3,1,2,0:T(8,128)(2,1)S(1)} fusion(bf16[4,8,128,2,128]{2,4,1,3,0:T(8,128)(2,1)} %copy-done.4, bf16[2,128,4,128,1]{1,3,2,0,4:T(8,128)(2,1)S(1)} %bitcast.118), kind=kOutput, calls=%fused_computation.11 | convolution fusion | flops 269484032 | bytes 3407872 | tf_op jit(solution)/shard_map/gaqjk,jkgh->qgah/dot_general | solution.py:36
  81.0 1.3 %copy.140 = bf16[128,4096]{1,0:T(8,128)(2,1)} copy(bf16[128,4096]{0,1:T(8,128)(2,1)S(1)} %bitcast.120) | data formatting | bytes 2097152
  82.4 1.3 %copy.139 = bf16[128,4096]{1,0:T(8,128)(2,1)} copy(bf16[128,4096]{0,1:T(8,128)(2,1)S(1)} %bitcast.110) | data formatting | bytes 2097152
  83.7 4.1 %all-to-all-done.3 = bf16[8,16,1024]{2,1,0:T(8,128)(2,1)S(1)} async-done(((bf16[8,16,1024]{2,1,0:T(8,128)(2,1)}), bf16[8,16,1024]{2,1,0:T(8,128)(2,1)S(1)}, u32[]{:S(2)}, u32[]{:S(2)}) %all-to-all-start.3) | async-done | bytes 262176 | tf_op jit(solution)/shard_map/all_to_all | solution.py:99
  87.8 0.7 slice_bitcast_fusion
  (13 shorter events, 0.2 us)
Async XLA Ops:
  0.6 26.4 %copy-start.1 = (bf16[128,4096]{1,0:T(8,128)(2,1)S(1)}, bf16[128,4096]{1,0:T(8,128)(2,1)}, u32[]{:S(2)}) copy-start(bf16[128,4096]{1,0:T(8,128)(2,1)} %param.11) | copy-start | bytes 3145732
  23.5 17.3 %all-to-all-start.1 = ((bf16[8,2,16,1024]{3,2,1,0:T(8,128)(2,1)}), bf16[8,2,16,1024]{3,2,1,0:T(8,128)(2,1)S(1)}, u32[]{:S(2)}, u32[]{:S(2)}) async-start(bf16[8,2,16,1024]{3,2,1,0:T(8,128)(2,1)} %bitcast.3), calls=%async_computation.1 | async-start | bytes 1048576 | tf_op jit(solution)/shard_map/all_to_all | solution.py:72
  42.9 2.1 %copy-start = (f32[4,2,128,128,8]{3,2,4,1,0:T(8,128)}, f32[4,2,128,128,8]{3,2,4,1,0:T(8,128)S(1)}, u32[]{:S(2)}) copy-start(f32[4,2,128,128,8]{3,2,4,1,0:T(8,128)S(1)} %get-tuple-element.45) | copy-start | bytes 12582916
  43.9 1.8 %copy-start.3 = (bf16[2,128,512]{1,2,0:T(8,128)(2,1)S(1)}, bf16[2,128,512]{1,2,0:T(8,128)(2,1)}, u32[]{:S(2)}) copy-start(bf16[2,128,512]{1,2,0:T(8,128)(2,1)} %copy.121) | copy-start | bytes 786436
  53.1 1.3 %copy-start.4 = (bf16[4,8,128,2,128]{2,4,1,3,0:T(8,128)(2,1)}, bf16[4,8,128,2,128]{2,4,1,3,0:T(8,128)(2,1)S(1)}, u32[]{:S(2)}) copy-start(bf16[4,8,128,2,128]{2,4,1,3,0:T(8,128)(2,1)S(1)} %fusion.1) | copy-start | bytes 6291460
  53.1 1.6 %copy-start.2 = (bf16[2,8,16,512]{3,2,1,0:T(8,128)(2,1)S(1)}, bf16[2,8,16,512]{3,2,1,0:T(8,128)(2,1)}, u32[]{:S(2)}) copy-start(bf16[2,8,16,512]{3,2,1,0:T(8,128)(2,1)} %concatenate.31) | copy-start | bytes 786436
  56.2 17.8 %all-to-all-start.2 = ((bf16[2,8,16,1024]{3,0,2,1:T(2,128)(2,1)}), bf16[2,8,16,1024]{3,0,2,1:T(2,128)(2,1)S(1)}, u32[]{:S(2)}, u32[]{:S(2)}) async-start(bf16[2,8,16,1024]{3,0,2,1:T(2,128)(2,1)} %copy.136), calls=%async_computation.2 | async-start | bytes 1048576 | tf_op jit(solution)/shard_map/all_to_all | solution.py:88
  75.3 12.5 %all-to-all-start.3 = ((bf16[8,16,1024]{2,1,0:T(8,128)(2,1)}), bf16[8,16,1024]{2,1,0:T(8,128)(2,1)S(1)}, u32[]{:S(2)}, u32[]{:S(2)}) async-start(bf16[8,16,1024]{2,1,0:T(8,128)(2,1)} %copy.138), calls=%async_computation.3 | async-start | bytes 524288 | tf_op jit(solution)/shard_map/all_to_all | solution.py:99
where the time goes:
time: 89.1 us; the launch traced here: 88.5 us
  waiting for transfers between devices  29.9 us (34%)
  blocking collectives  17.4 us (20%)
  local copies, waits for them, and re-layouts  13.9 us (16%)
  starting transfers between devices  10.8 us (12%)
  matrix products  9.43 us (11%)
  other arithmetic  5.54 us (6%)
  between operations  1.53 us (2%)
    all_to_all x1, blocking collectives, shards(): first_recv = lax.all_to_all(first_send, 'ctx', 0, 0, tiled=True)  17.4 us
    all_to_all x1, waiting for transfers between devices, shards(): lax.all_to_all(pieces.reshape(LIST, peers, chunk_rows, both_width), 'ctx'...  14.2 us
    all_to_all x1, waiting for transfers between devices, shards(): fetched = lax.all_to_all(picked, 'ctx', 0, 2, tiled=True)[0]  11.6 us
    unnamed x16, local copies, waits for them, and re-layouts  5.36 us
    all_to_all x1, waiting for transfers between devices, shards(): lax.all_to_all(summed, 'ctx', 0, 0, tiled=True)  4.13 us
    dot_general x1, matrix products, attend(): jnp.einsum('qgah,jkgh->gaqjk', grad_part, value_part, preferred_element_t...  3.92 us
    all_to_all x1, starting transfers between devices, shards(): lax.all_to_all(pieces.reshape(LIST, peers, chunk_rows, both_width), 'ctx'...  3.64 us
    all_to_all x1, starting transfers between devices, shards(): lax.all_to_all(summed, 'ctx', 0, 0, tiled=True)  3.63 us
  transfers between devices with their start and end apart: 3, of which 3 were waited for; matrix products, arithmetic and copies ran while one was open for 8% of the time, Pallas kernels for 0%

commit v1 on v0

--- a/solution.py
+++ b/solution.py
@@ -8,6 +8,18 @@
 HEAD_SIZE = 128
 LIST = 2
 TAG_COLUMNS = 128
+
+
+def cells_trace(work_x, k_dim, on_dim=1):
+    return jnp.concatenate(
+        lax.all_to_all(
+            jnp.stack(jnp.split(work_x, lax.axis_size("ctx"), axis=k_dim)),
+            axis_name="ctx",
+            split_axis=0,
+            concat_axis=0,
+        ),
+        axis=on_dim,
+    )
 
 
 def attend(query_part, key_part, value_part, grad_part, live_slots):
@@ -85,9 +97,7 @@
             ],
             axis=2,
         ).astype(jnp.bfloat16)
-        back = lax.all_to_all(
-            pieces.reshape(LIST, peers, chunk_rows, both_width), "ctx", 1, 1, tiled=True
-        )
+        back = cells_trace(pieces.reshape(LIST, peers, chunk_rows, both_width), 1)
         slot_live = jnp.arange(LIST, dtype=jnp.int32)[None, :] < counts_all[:, None]
         selector = (
             (lists_all[:, :, None] == jnp.arange(peers, dtype=jnp.int32)[None, None, :])

time: 89.1 us -> 89.2 us (level)
    another operation x0 -> x2, local copies, waits for them, and re-layouts: none -> 1.34 us  [cells_trace(): jnp.stack(jnp.split(work_x, lax.axis_size('ctx'), axis=k_dim))]
    concatenate x3, local copies, waits for them, and re-layouts: 3.18 us -> 1.87 us  [shards(): jnp.concatenate([key_piece.reshape(LIST, row_count, key_width), value_pie...]
    unnamed x16 -> x24, local copies, waits for them, and re-layouts: 5.36 us -> 5.43 us
where the time goes in v1:
time: 89.2 us; the launch traced here: 88.6 us
  waiting for transfers between devices  29.9 us (34%)
  blocking collectives  17.4 us (20%)
  local copies, waits for them, and re-layouts  14 us (16%)
  starting transfers between devices  10.8 us (12%)
  matrix products  9.45 us (11%)
  other arithmetic  5.48 us (6%)
  between operations  1.6 us (2%)
    all_to_all x1, blocking collectives, shards(): first_recv = lax.all_to_all(first_send, 'ctx', 0, 0, tiled=True)  17.4 us
    all_to_all x1, waiting for transfers between devices, cells_trace(): lax.all_to_all(jnp.stack(jnp.split(work_x, lax.axis_size('ctx'), axis=k_d...  14.2 us
    all_to_all x1, waiting for transfers between devices, shards(): fetched = lax.all_to_all(picked, 'ctx', 0, 2, tiled=True)[0]  11.6 us
    unnamed x24, local copies, waits for them, and re-layouts  5.43 us
    all_to_all x1, waiting for transfers between devices, shards(): lax.all_to_all(summed, 'ctx', 0, 0, tiled=True)  4.13 us
    dot_general x1, matrix products, attend(): jnp.einsum('qgah,jkgh->gaqjk', grad_part, value_part, preferred_element_t...  3.92 us
    all_to_all x1, starting transfers between devices, cells_trace(): lax.all_to_all(jnp.stack(jnp.split(work_x, lax.axis_size('ctx'), axis=k_d...  3.63 us
    all_to_all x1, starting transfers between devices, shards(): lax.all_to_all(summed, 'ctx', 0, 0, tiled=True)  3.63 us
  transfers between devices with their start and end apart: 3, of which 3 were waited for; matrix products, arithmetic and copies ran while one was open for 8% of the time, Pallas kernels for 0%

profile of v1, /device:TPU:0, one launch (start us, length us, event | category | flops | bytes accessed | tf_op | source)
XLA Modules:
  0.0 88.6 jit_solution(13531339385126337616)
XLA Ops:
  0.6 0.0 copy-start.1
  0.6 0.6 compare_reduce_fusion
  1.9 0.7 convert_bitcast_fusion
  2.6 0.7 broadcast_select_fusion
  3.3 1.0 %maximum_maximum_fusion = bf16[8,16,1152]{2,1,0:T(8,128)(2,1)S(1)} fusion(bf16[8,16,512]{2,1,0:T(8,128)(2,1)} %bitcast.161, bf16[8,16,512]{2,1,0:T(8,128)(2,1)} %bitcast.162, bf16[1152]{0:T(1024)(128)(2,1)S(1)} %fusion.43), kind=kLoop, calls=%fused_computation.33 | loop fusion | flops 884736 | bytes 559360 | tf_op jit(solution)/shard_map/concatenate | solution.py:75
  4.4 17.4 %all_to_all.30 = bf16[8,16,1152]{2,1,0:T(8,128)(2,1)S(1)} all-to-all(bf16[8,16,1152]{2,1,0:T(8,128)(2,1)S(1)} %maximum_maximum_fusion), channel_id=1, replica_groups=mesh['parts'=2,'ctx'=8,'tp'=2] {'ctx'}, dimensions={0} | all-to-all | bytes 589824 | tf_op jit(solution)/shard_map/all_to_all | solution.py:78
  21.8 0.1 copy.426
  21.9 0.1 copy.370
  22.0 0.1 reshape.119
  22.1 1.4 %gather_fusion = bf16[16,16,1024]{2,1,0:T(8,128)(2,1)} fusion(bf16[8,16,1024]{2,1,0:T(8,128)(2,1)S(1)} %slice.53, s32[1024]{0:T(1024)S(1)} %pad_clamp_fusion), kind=kCustom, calls=%fused_computation | custom fusion | bytes 1048640 | tf_op jit(solution)/shard_map/jit(_take)/gather | solution.py:83
  23.5 3.5 %all-to-all-start.1 = ((bf16[8,2,16,1024]{3,2,1,0:T(8,128)(2,1)}), bf16[8,2,16,1024]{3,2,1,0:T(8,128)(2,1)S(1)}, u32[]{:S(2)}, u32[]{:S(2)}) async-start(bf16[8,2,16,1024]{3,2,1,0:T(8,128)(2,1)} %bitcast.3), calls=%async_computation.1 | async-start | bytes 1048576 | tf_op jit(solution)/shard_map/all_to_all | solution.py:84
  27.0 0.0 copy-done.1
  27.0 0.7 copy.378
  27.7 1.4 %copy.427 = bf16[16,8,32,128]{3,2,1,0:T(8,128)(2,1)S(1)} copy(bf16[16,8,32,128]{3,1,2,0:T(8,128)(2,1)} %bitcast.156) | data formatting | bytes 2097152
  29.1 11.6 %all-to-all-done.1 = bf16[8,2,16,1024]{3,2,1,0:T(8,128)(2,1)S(1)} async-done(((bf16[8,2,16,1024]{3,2,1,0:T(8,128)(2,1)}), bf16[8,2,16,1024]{3,2,1,0:T(8,128)(2,1)S(1)}, u32[]{:S(2)}, u32[]{:S(2)}) %all-to-all-start.1) | async-done | bytes 524320 | tf_op jit(solution)/shard_map/all_to_all | solution.py:84
  40.8 0.8 copy.372
  41.7 0.2 copy.373
  41.9 1.1 %bitcast_reduce_fusion = (f32[4,8,128]{2,1,0:T(8,128)S(1)}, f32[4,2,128,128,8]{3,2,4,1,0:T(8,128)S(1)}) fusion(pred[2]{0:T(512)(128)(4,1)S(1)} %iota_compare_fusion.3, bf16[128,4,8,128,1]{3,2,1,0,4:T(8,128)(2,1)S(1)} %bitcast.150, bf16[2,128,4,128,1]{1,3,2,0,4:T(8,128)(2,1)S(1)} %bitcast.154), kind=kOutput, calls=%fused_computation.5 | convolution fusion | flops 271577088 | bytes 5521410 | tf_op jit(solution)/shard_map/qgah,jkgh->gaqjk/dot_general | solution.py:27
  42.9 0.0 copy-start
  42.9 1.0 %fusion.4 = f32[4,8,128]{2,1,0:T(8,128)S(1)} fusion(f32[4,2,128,128,8]{3,2,4,1,0:T(8,128)S(1)} %get-tuple-element.73, f32[4,8,128]{2,1,0:T(8,128)S(1)} %get-tuple-element.72, pred[2]{0:T(512)(128)(4,1)S(1)} %iota_compare_fusion.3), kind=kLoop, calls=%fused_computation.9 | loop fusion | flops 4190208 | bytes 4227074 | tf_op jit(solution)/shard_map/reduce_sum | solution.py:33
  43.9 0.0 copy-start.3
  43.9 1.1 %fusion.46 = bf16[4,8,128,2,128]{2,4,1,3,0:T(8,128)(2,1)S(1)} fusion(f32[4,8,128]{2,1,0:T(8,128)S(1)} %fusion.4, f32[4,8,128]{2,1,0:T(8,128)S(1)} %get-tuple-element.72, f32[4,2,128,128,8]{3,2,4,1,0:T(8,128)S(1)} %get-tuple-element.73, pred[2]{0:T(512)(128)(4,1)S(1)} %iota_compare_fusion.3), kind=kLoop, calls=%fused_computation.73 | loop fusion | flops 5242880 | bytes 6324226 | tf_op jit(solution)/shard_map/convert_element_type | solution.py:34
  45.0 0.0 copy-done
  45.0 0.7 fusion.21
  45.7 0.0 copy-done.3
  45.7 0.5 fusion.14
  46.2 0.9 %copy.386 = bf16[2,128,4,128]{3,2,1,0:T(4,128)(2,1)} copy(bf16[2,128,4,128]{3,1,0,2:T(8,128)(2,1)S(1)} %fusion.21) | data formatting | bytes 524288 | tf_op jit(solution)/shard_map/gaqjk,qgah->jkgh/transpose | solution.py:53
  47.1 1.7 %concatenate.31 = bf16[2,8,16,512]{3,2,1,0:T(8,128)(2,1)} reshape(bf16[2,128,4,128]{3,2,1,0:T(4,128)(2,1)} %copy.386) | data formatting | bytes 524288 | tf_op jit(solution)/shard_map/concatenate | solution.py:93
  48.8 0.4 multiply_reduce_fusion
  49.2 3.9 %fusion.1 = bf16[4,8,128,2,128]{2,4,1,3,0:T(8,128)(2,1)S(1)} fusion(bf16[128,4,8,128,1]{0,3,2,4,1:T(8,128)(2,1)S(1)} %bitcast.149, f32[4,8,128]{2,1,0:T(8,128)S(1)} %bitcast.163, bf16[2,128,4,128,1]{1,3,2,0,4:T(8,128)(2,1)} %bitcast.159, f32[4,8,128]{2,1,0:T(8,128)S(1)} %fusion.4, f32[4,8,128]{2,1,0:T(8,128)S(1)} %get-tuple-element.72, ...), kind=kOutput, calls=%fused_computation.3 | convolution fusion | flops 275775488 | bytes 7651330 | tf_op jit(solution)/shard_map/qgah,jkgh->gaqjk/dot_general | solution.py:40
  53.1 0.0 copy-start.4
  53.2 0.0 copy-start.2
  53.2 0.8 fusion.22
  54.0 0.5 copy-done.4
  54.5 0.2 copy.384
  54.7 0.1 concatenate.30
  54.8 0.0 copy-done.2
  55.0 1.3 %copy.387 = bf16[8,2,1,16,1024]{4,1,3,2,0:T(2,128)(2,1)} copy(bf16[8,2,1,16,1024]{4,3,1,2,0:T(8,128)(2,1)S(1)} %fusion.32) | data formatting | bytes 1048576 | tf_op jit(solution)/shard_map/stack | solution.py:16
  56.3 3.6 %all-to-all-start.2 = ((bf16[8,2,1,16,1024]{4,1,3,2,0:T(2,128)(2,1)}), bf16[8,2,1,16,1024]{4,1,3,2,0:T(2,128)(2,1)S(1)}, u32[]{:S(2)}, u32[]{:S(2)}) async-start(bf16[8,2,1,16,1024]{4,1,3,2,0:T(2,128)(2,1)} %copy.387), calls=%async_computation.2 | async-start | bytes 1048576 | tf_op jit(solution)/shard_map/all_to_all | solution.py:15
  60.0 14.2 %all-to-all-done.2 = bf16[8,2,1,16,1024]{4,1,3,2,0:T(2,128)(2,1)S(1)} async-done(((bf16[8,2,1,16,1024]{4,1,3,2,0:T(2,128)(2,1)}), bf16[8,2,1,16,1024]{4,1,3,2,0:T(2,128)(2,1)S(1)}, u32[]{:S(2)}, u32[]{:S(2)}) %all-to-all-start.2) | async-done | bytes 524320 | tf_op jit(solution)/shard_map/all_to_all | solution.py:15
  74.1 0.4 fusion.20
  74.5 0.9 copy.389
  75.4 3.6 %all-to-all-start.3 = ((bf16[8,16,1024]{2,1,0:T(8,128)(2,1)}), bf16[8,16,1024]{2,1,0:T(8,128)(2,1)S(1)}, u32[]{:S(2)}, u32[]{:S(2)}) async-start(bf16[8,16,1024]{2,1,0:T(8,128)(2,1)} %copy.389), calls=%async_computation.3 | async-start | bytes 524288 | tf_op jit(solution)/shard_map/all_to_all | solution.py:109
  79.0 2.1 %fusion.5 = bf16[4,128,8,128]{3,1,2,0:T(8,128)(2,1)S(1)} fusion(bf16[4,8,128,2,128]{2,4,1,3,0:T(8,128)(2,1)} %copy-done.4, bf16[2,128,4,128,1]{1,3,2,0,4:T(8,128)(2,1)S(1)} %bitcast.155), kind=kOutput, calls=%fused_computation.11 | convolution fusion | flops 269484032 | bytes 3407872 | tf_op jit(solution)/shard_map/gaqjk,jkgh->qgah/dot_general | solution.py:48
  81.2 1.3 %copy.391 = bf16[128,4096]{1,0:T(8,128)(2,1)} copy(bf16[128,4096]{0,1:T(8,128)(2,1)S(1)} %bitcast.157) | data formatting | bytes 2097152
  82.5 1.3 %copy.390 = bf16[128,4096]{1,0:T(8,128)(2,1)} copy(bf16[128,4096]{0,1:T(8,128)(2,1)S(1)} %bitcast.147) | data formatting | bytes 2097152
  83.8 4.1 %all-to-all-done.3 = bf16[8,16,1024]{2,1,0:T(8,128)(2,1)S(1)} async-done(((bf16[8,16,1024]{2,1,0:T(8,128)(2,1)}), bf16[8,16,1024]{2,1,0:T(8,128)(2,1)S(1)}, u32[]{:S(2)}, u32[]{:S(2)}) %all-to-all-start.3) | async-done | bytes 262176 | tf_op jit(solution)/shard_map/all_to_all | solution.py:109
  87.9 0.7 slice_bitcast_fusion
  (22 shorter events, 0.3 us)
Async XLA Ops:
  0.6 26.4 %copy-start.1 = (bf16[128,4096]{1,0:T(8,128)(2,1)S(1)}, bf16[128,4096]{1,0:T(8,128)(2,1)}, u32[]{:S(2)}) copy-start(bf16[128,4096]{1,0:T(8,128)(2,1)} %param.11) | copy-start | bytes 3145732
  23.5 17.3 %all-to-all-start.1 = ((bf16[8,2,16,1024]{3,2,1,0:T(8,128)(2,1)}), bf16[8,2,16,1024]{3,2,1,0:T(8,128)(2,1)S(1)}, u32[]{:S(2)}, u32[]{:S(2)}) async-start(bf16[8,2,16,1024]{3,2,1,0:T(8,128)(2,1)} %bitcast.3), calls=%async_computation.1 | async-start | bytes 1048576 | tf_op jit(solution)/shard_map/all_to_all | solution.py:84
  42.9 2.1 %copy-start = (f32[4,2,128,128,8]{3,2,4,1,0:T(8,128)}, f32[4,2,128,128,8]{3,2,4,1,0:T(8,128)S(1)}, u32[]{:S(2)}) copy-start(f32[4,2,128,128,8]{3,2,4,1,0:T(8,128)S(1)} %get-tuple-element.73) | copy-start | bytes 12582916
  43.9 1.8 %copy-start.3 = (bf16[2,128,512]{1,2,0:T(8,128)(2,1)S(1)}, bf16[2,128,512]{1,2,0:T(8,128)(2,1)}, u32[]{:S(2)}) copy-start(bf16[2,128,512]{1,2,0:T(8,128)(2,1)} %copy.372) | copy-start | bytes 786436
  53.1 1.3 %copy-start.4 = (bf16[4,8,128,2,128]{2,4,1,3,0:T(8,128)(2,1)}, bf16[4,8,128,2,128]{2,4,1,3,0:T(8,128)(2,1)S(1)}, u32[]{:S(2)}) copy-start(bf16[4,8,128,2,128]{2,4,1,3,0:T(8,128)(2,1)S(1)} %fusion.1) | copy-start | bytes 6291460
  53.2 1.7 %copy-start.2 = (bf16[2,8,16,512]{3,2,1,0:T(8,128)(2,1)S(1)}, bf16[2,8,16,512]{3,2,1,0:T(8,128)(2,1)}, u32[]{:S(2)}) copy-start(bf16[2,8,16,512]{3,2,1,0:T(8,128)(2,1)} %concatenate.31) | copy-start | bytes 786436
  56.3 17.8 %all-to-all-start.2 = ((bf16[8,2,1,16,1024]{4,1,3,2,0:T(2,128)(2,1)}), bf16[8,2,1,16,1024]{4,1,3,2,0:T(2,128)(2,1)S(1)}, u32[]{:S(2)}, u32[]{:S(2)}) async-start(bf16[8,2,1,16,1024]{4,1,3,2,0:T(2,128)(2,1)} %copy.387), calls=%async_computation.2 | async-start | bytes 1048576 | tf_op jit(solution)/shard_map/all_to_all | solution.py:15
  75.4 12.5 %all-to-all-start.3 = ((bf16[8,16,1024]{2,1,0:T(8,128)(2,1)}), bf16[8,16,1024]{2,1,0:T(8,128)(2,1)S(1)}, u32[]{:S(2)}, u32[]{:S(2)}) async-start(bf16[8,16,1024]{2,1,0:T(8,128)(2,1)} %copy.389), calls=%async_computation.3 | async-start | bytes 524288 | tf_op jit(solution)/shard_map/all_to_all | solution.py:109
